TPU v7x, 32 devices: a whole 2x2x4 slice. The times are simulated.
32 devices in a mesh: row: 8 (over z, core), col: 4 (over y, x).
Axes of the slice: x: 2, y: 2, z: 4, core: 2. Of those that a mesh axis runs over, the one named last changes fastest.
Arguments:
- activations: bfloat16 [1024, 8192], P('col', 'row'), may hold values from -6 to 6
- out_grad: bfloat16 [1024, 8192], P('col', 'row'), may hold values from -6 to 6
- gate_pre: bfloat16 [1024, 16384], P('row', 'col'), may hold values from -8 to 8
- up_proj: bfloat16 [1024, 16384], P('row', 'col'), may hold values from -6 to 6
- gate_weight: bfloat16 [8192, 16384], P('row', 'col'), may hold values from -0.0625 to 0.0625
- up_weight: bfloat16 [8192, 16384], P('row', 'col'), may hold values from -0.0625 to 0.0625
- down_weight: bfloat16 [16384, 8192], P('col', 'row'), may hold values from -0.046875 to 0.046875
Outputs:
- input_grad: bfloat16 [1024, 8192], P('col', 'row')
- gate_grad: bfloat16 [8192, 16384], P('row', 'col')
- up_grad: bfloat16 [8192, 16384], P('row', 'col')
- down_grad: bfloat16 [16384, 8192], P('col', 'row')
All inputs are finite; a program needn't handle non-finite values.
Results may differ from a plain program's by a relative error of at most 0.0051.
Values may be sent and summed in bfloat16 or wider, within the bound.
No kernel may reach another device: no remote copies, remote signals or barrier semaphores. Data moves between devices by JAX's collectives and lax.ppermute only.
A program may use at most 192 MiB of HBM per device.

v0:
```python
import jax
import jax.numpy as jnp
from jax import lax
from jax.sharding import PartitionSpec as P


def local_grads(gate_rows, up_rows, grad_rows):
    gate_float = gate_rows.astype(jnp.float32)
    up_float = up_rows.astype(jnp.float32)
    sigmoid_gate = jax.nn.sigmoid(gate_float)
    silu_gate = gate_float * sigmoid_gate
    hidden_act = (silu_gate * up_float).astype(jnp.bfloat16)
    gate_delta = (
        grad_rows * up_float * sigmoid_gate * (1.0 + gate_float * (1.0 - sigmoid_gate))
    ).astype(jnp.bfloat16)
    up_delta = (grad_rows * silu_gate).astype(jnp.bfloat16)
    return (hidden_act, gate_delta, up_delta)


def body(activations, out_grad, gate_pre, up_proj, gate_weight, up_weight, down_weight):
    act_full, grad_full = (
        lax.all_gather(activations, "col", axis=0, tiled=True),
        lax.all_gather(out_grad, "col", axis=0, tiled=True),
    )
    tokens_all = act_full.shape[0]
    contract_last = (((1,), (1,)), ((), ()))
    contract_first = (((0,), (0,)), ((), ()))
    grad_rows = grad_full
    hid_rows = lax.psum_scatter(
        lax.dot_general(grad_rows, down_weight, contract_last, preferred_element_type=jnp.float32),
        "row",
        scatter_dimension=0,
        tiled=True,
    )
    products = local_grads(gate_pre, up_proj, hid_rows)
    hidden_act = lax.all_gather(products[0], "row", axis=0, tiled=True)
    gate_delta = lax.all_gather(products[1], "row", axis=0, tiled=True)
    up_delta = lax.all_gather(products[2], "row", axis=0, tiled=True)
    grad_rows = grad_full
    acc_down = lax.dot_general(
        hidden_act, grad_rows, contract_first, preferred_element_type=jnp.float32
    )
    acc_gate = lax.dot_general(
        act_full, gate_delta, contract_first, preferred_element_type=jnp.float32
    )
    acc_up = lax.dot_general(act_full, up_delta, contract_first, preferred_element_type=jnp.float32)
    input_rows = lax.dot_general(
        gate_delta, gate_weight, contract_last, preferred_element_type=jnp.float32
    )
    input_rows = input_rows + lax.dot_general(
        up_delta, up_weight, contract_last, preferred_element_type=jnp.float32
    )
    acc_input = input_rows
    totals = (acc_down, acc_gate, acc_up, acc_input)
    acc_down, acc_gate, acc_up, acc_input = totals
    input_rows = lax.psum_scatter(acc_input, "col", scatter_dimension=0, tiled=True).astype(
        jnp.bfloat16
    )
    factor = float(tokens_all) ** (-0.5)
    return (
        input_rows,
        (acc_gate * factor).astype(jnp.bfloat16),
        (acc_up * factor).astype(jnp.bfloat16),
        (acc_down * factor).astype(jnp.bfloat16),
    )


def solution(mesh):
    in_specs = (
        P("col", "row"),
        P("col", "row"),
        P("row", "col"),
        P("row", "col"),
        P("row", "col"),
        P("row", "col"),
        P("col", "row"),
    )
    out_specs = (P("col", "row"), P("row", "col"), P("row", "col"), P("col", "row"))
    return jax.shard_map(body, mesh=mesh, in_specs=in_specs, out_specs=out_specs, check_vma=False)
```

profile of v0, /device:TPU:0, one launch (start us, length us, event | category | flops | bytes accessed | tf_op | source)
XLA Modules:
  0.0 582.2 jit_solution(11149804209979248327)
XLA Ops:
  7.2 0.0 all-gather.6.cloned.1.call-start
  7.2 0.7 all-gather.6.cloned.1.call-update
  7.9 0.0 reduce-scatter.3.cloned.1.call-start
  7.9 39.9 %all-gather.6.cloned.1.call-done = bf16[1024,1024]{1,0:T(8,128)(2,1)} async-done(((bf16[256,1024]{1,0:T(8,128)(2,1)}), bf16[1024,1024]{1,0:T(8,128)(2,1)}) %all-gather.6.cloned.1.call-update) | async-done | bytes 2097168 | tf_op jit(solution)/shard_map/all_gather | solution.py:23
  47.9 16.0 %fusion.10 = f32[1024,4096]{1,0:T(8,128)} fusion(bf16[1024,1024]{1,0:T(8,128)(2,1)} %all-gather.6.cloned.1.call-done, bf16[4096,1024]{1,0:T(8,128)(2,1)} %param.13), kind=kOutput, calls=%fused_computation.20 | convolution fusion | flops 8589934592 | bytes 27262976 | tf_op jit(solution)/shard_map/dot_general | solution.py:30
  63.9 0.0 reduce-scatter.3.cloned.1.call-update
  64.0 0.0 all-gather.8.cloned.1.call-start
  64.0 168.3 %reduce-scatter.3.cloned.1.call-done = f32[128,4096]{1,0:T(8,128)} async-done(((f32[1024,4096]{1,0:T(8,128)}), f32[128,4096]{1,0:T(8,128)}) %reduce-scatter.3.cloned.1.call-update) | async-done | bytes 2097168 | tf_op jit(solution)/shard_map/reduce_scatter | solution.py:29
  232.4 0.0 copy-done
  232.4 4.4 multiply_convert_fusion.3
  236.7 0.0 all-gather.8.cloned.1.call-update
  236.8 0.0 all-gather.10.cloned.1.call-start
  236.8 0.5 all-gather.10.cloned.1.call-update
  237.3 0.0 all-gather.12.cloned.1.call-start
  237.4 0.5 all-gather.12.cloned.1.call-update
  237.9 0.0 all-gather.14.cloned.1.call-start
  238.0 0.5 all-gather.14.cloned.1.call-update
  238.5 0.2 reduce-scatter.5.cloned.1.call-start
  238.7 78.6 %all-gather.8.cloned.1.call-done = bf16[1024,4096]{1,0:T(8,128)(2,1)} async-done(((bf16[128,4096]{1,0:T(8,128)(2,1)}), bf16[1024,4096]{1,0:T(8,128)(2,1)}) %all-gather.8.cloned.1.call-update) | async-done | bytes 8388624 | tf_op jit(solution)/shard_map/all_gather | solution.py:37
  317.3 15.0 %fusion.11 = f32[1024,1024]{1,0:T(8,128)} fusion(bf16[1024,4096]{1,0:T(8,128)(2,1)} %all-gather.8.cloned.1.call-done, bf16[1024,4096]{1,0:T(8,128)(2,1)} %param.11), kind=kOutput, calls=%fused_computation.21 | convolution fusion | flops 8589934592 | bytes 20971520 | tf_op jit(solution)/shard_map/dot_general | solution.py:47
  332.3 67.6 %all-gather.10.cloned.1.call-done = bf16[1024,4096]{1,0:T(8,128)(2,1)} async-done(((bf16[128,4096]{1,0:T(8,128)(2,1)}), bf16[1024,4096]{1,0:T(8,128)(2,1)}) %all-gather.10.cloned.1.call-update) | async-done | bytes 8388624 | tf_op jit(solution)/shard_map/all_gather | solution.py:38
  400.0 15.7 %convolution_add_fusion = f32[1024,1024]{1,0:T(8,128)} fusion(f32[1024,1024]{1,0:T(8,128)} %fusion.11, bf16[1024,4096]{1,0:T(8,128)(2,1)} %all-gather.10.cloned.1.call-done, bf16[1024,4096]{1,0:T(8,128)(2,1)} %param.12), kind=kOutput, calls=%fused_computation.19 | convolution fusion | flops 8590983168 | bytes 25165824 | tf_op jit(solution)/shard_map/dot_general | solution.py:50
  415.7 0.0 reduce-scatter.5.cloned.1.call-update
  415.7 19.8 %all-gather.12.cloned.1.call-done = bf16[1024,1024]{1,0:T(8,128)(2,1)} async-done(((bf16[256,1024]{1,0:T(8,128)(2,1)}), bf16[1024,1024]{1,0:T(8,128)(2,1)}) %all-gather.12.cloned.1.call-update) | async-done | bytes 2097168 | tf_op jit(solution)/shard_map/all_gather | solution.py:22
  435.5 14.9 %fusion = bf16[1024,4096]{0,1:T(8,128)(2,1)} fusion(bf16[1024,4096]{1,0:T(8,128)(2,1)} %all-gather.8.cloned.1.call-done, bf16[1024,1024]{1,0:T(8,128)(2,1)} %all-gather.12.cloned.1.call-done), kind=kOutput, calls=%fused_computation.3 | convolution fusion | flops 8598323200 | bytes 18874368 | tf_op jit(solution)/shard_map/dot_general | solution.py:43
  450.4 12.1 %copy.11 = bf16[1024,4096]{1,0:T(8,128)(2,1)} copy(bf16[1024,4096]{0,1:T(8,128)(2,1)} %fusion) | data formatting | bytes 16777216
  462.5 14.7 %fusion.1 = bf16[1024,4096]{0,1:T(8,128)(2,1)} fusion(bf16[1024,4096]{1,0:T(8,128)(2,1)} %all-gather.10.cloned.1.call-done, bf16[1024,1024]{1,0:T(8,128)(2,1)S(1)} %copy-done.3), kind=kOutput, calls=%fused_computation.4 | convolution fusion | flops 8598323200 | bytes 18874368 | tf_op jit(solution)/shard_map/dot_general | solution.py:46
  477.2 12.1 %copy.12 = bf16[1024,4096]{1,0:T(8,128)(2,1)} copy(bf16[1024,4096]{0,1:T(8,128)(2,1)} %fusion.1) | data formatting | bytes 16777216
  489.3 29.8 %all-gather.14.cloned.1.call-done = bf16[1024,4096]{1,0:T(8,128)(2,1)} async-done(((bf16[128,4096]{1,0:T(8,128)(2,1)}), bf16[1024,4096]{1,0:T(8,128)(2,1)}) %all-gather.14.cloned.1.call-update) | async-done | bytes 8388624 | tf_op jit(solution)/shard_map/all_gather | solution.py:36
  519.1 14.6 %multiply_convert_fusion = bf16[4096,1024]{1,0:T(8,128)(2,1)} fusion(bf16[1024,4096]{1,0:T(8,128)(2,1)} %all-gather.14.cloned.1.call-done, bf16[1024,1024]{1,0:T(8,128)(2,1)S(1)} %copy-done.2), kind=kOutput, calls=%fused_computation | convolution fusion | flops 8598323200 | bytes 18874368 | tf_op jit(solution)/shard_map/dot_general | solution.py:40
  533.6 39.7 %reduce-scatter.5.cloned.1.call-done = f32[256,1024]{1,0:T(8,128)} async-done(((f32[1024,1024]{1,0:T(8,128)}), f32[256,1024]{1,0:T(8,128)}) %reduce-scatter.5.cloned.1.call-update) | async-done | bytes 1048592 | tf_op jit(solution)/shard_map/reduce_scatter | solution.py:56
  573.3 2.1 convert_element_type.37
  (7 shorter events, 0.0 us)
Async XLA Ops:
  7.2 40.7 %all-gather.6.cloned.1.call-start = ((), (), s32[]{:S(2)}) async-start(), calls=%async_computation.2 | async-start | bytes 2621440 | tf_op jit(solution)/shard_map/all_gather | solution.py:23
  7.9 224.5 %reduce-scatter.3.cloned.1.call-start = ((), (), s32[]{:S(2)}) async-start(), calls=%async_computation.3 | async-start | bytes 18874368 | tf_op jit(solution)/shard_map/reduce_scatter | solution.py:29
  63.9 168.4 %copy-start = (bf16[128,4096]{1,0:T(8,128)(2,1)S(1)}, bf16[128,4096]{1,0:T(8,128)(2,1)}, u32[]{:S(2)}) copy-start(bf16[128,4096]{1,0:T(8,128)(2,1)} %param.9) | copy-start | bytes 3145732
  63.9 168.4 %copy-start.1 = (bf16[128,4096]{1,0:T(8,128)(2,1)S(1)}, bf16[128,4096]{1,0:T(8,128)(2,1)}, u32[]{:S(2)}) copy-start(bf16[128,4096]{1,0:T(8,128)(2,1)} %param.10) | copy-start | bytes 3145732
  64.0 253.3 %all-gather.8.cloned.1.call-start = ((), (), s32[]{:S(2)}) async-start(), calls=%async_computation.4 | async-start | bytes 9437184 | tf_op jit(solution)/shard_map/all_gather | solution.py:37
  236.8 163.2 %all-gather.10.cloned.1.call-start = ((), (), s32[]{:S(2)}) async-start(), calls=%async_computation.5 | async-start | bytes 9437184 | tf_op jit(solution)/shard_map/all_gather | solution.py:38
  237.3 198.2 %all-gather.12.cloned.1.call-start = ((), (), s32[]{:S(2)}) async-start(), calls=%async_computation.7 | async-start | bytes 2621440 | tf_op jit(solution)/shard_map/all_gather | solution.py:22
  237.9 281.1 %all-gather.14.cloned.1.call-start = ((), (), s32[]{:S(2)}) async-start(), calls=%async_computation.8 | async-start | bytes 9437184 | tf_op jit(solution)/shard_map/all_gather | solution.py:36
  238.5 334.8 %reduce-scatter.5.cloned.1.call-start = ((), (), s32[]{:S(2)}) async-start(), calls=%async_computation.6 | async-start | bytes 5242880 | tf_op jit(solution)/shard_map/reduce_scatter | solution.py:56
  450.4 12.1 %copy-start.3 = (bf16[1024,1024]{1,0:T(8,128)(2,1)S(1)}, bf16[1024,1024]{1,0:T(8,128)(2,1)}, u32[]{:S(2)}) copy-start(bf16[1024,1024]{1,0:T(8,128)(2,1)} %all-gather.12.cloned.1.call-done) | copy-start | bytes 6291460
  477.2 41.9 %copy-start.2 = (bf16[1024,1024]{1,0:T(8,128)(2,1)S(1)}, bf16[1024,1024]{1,0:T(8,128)(2,1)}, u32[]{:S(2)}) copy-start(bf16[1024,1024]{1,0:T(8,128)(2,1)} %all-gather.6.cloned.1.call-done) | copy-start | bytes 6291460
Sparse Core Ops, SparseCore 0:
  9.8 38.0 all-gather.5
  64.1 168.2 reduce-scatter.2
  236.9 80.3 all-gather.7
  319.3 80.5 all-gather.9
  401.6 33.8 all-gather.11
  437.0 82.0 all-gather.13
  522.0 51.2 reduce-scatter.4
where the time goes:
time: 583 us; the launch traced here: 582 us
  waiting for transfers between devices  446 us (77%)
  matrix products  90.9 us (16%)
  local copies, waits for them, and re-layouts  24.2 us (4%)
  between operations  14.1 us (2%)
  other arithmetic  6.46 us (1%)
    reduce_scatter x1, waiting for transfers between devices, body(): lax.psum_scatter(lax.dot_general(grad_rows, down_weight, contract_last, p...  168 us
    all_gather x1, waiting for transfers between devices, body(): gate_delta = lax.all_gather(products[1], 'row', axis=0, tiled=True)  78.6 us
    all_gather x1, waiting for transfers between devices, body(): up_delta = lax.all_gather(products[2], 'row', axis=0, tiled=True)  67.6 us
    all_gather x1, waiting for transfers between devices, body(): lax.all_gather(out_grad, 'col', axis=0, tiled=True)  39.9 us
    reduce_scatter x1, waiting for transfers between devices, body(): lax.psum_scatter(acc_input, 'col', scatter_dimension=0, tiled=True)  39.7 us
    all_gather x1, waiting for transfers between devices, body(): hidden_act = lax.all_gather(products[0], 'row', axis=0, tiled=True)  29.8 us
    unnamed x10, local copies, waits for them, and re-layouts  24.2 us
    all_gather x1, waiting for transfers between devices, body(): lax.all_gather(activations, 'col', axis=0, tiled=True)  19.8 us
  transfers between devices with their start and end apart: 7, of which 7 were waited for; matrix products, arithmetic and copies ran while one was open for 17% of the time, Pallas kernels for 0%

commit v1 on v0

--- a/solution.py
+++ b/solution.py
@@ -35,7 +35,12 @@
     products = local_grads(gate_pre, up_proj, hid_rows)
     hidden_act = lax.all_gather(products[0], "row", axis=0, tiled=True)
     gate_delta = lax.all_gather(products[1], "row", axis=0, tiled=True)
-    up_delta = lax.all_gather(products[2], "row", axis=0, tiled=True)
+    ring = [products[2]]
+    for hop in range(7):
+        ring.append(lax.ppermute(ring[-1], "row", [(dev, (dev + 1) % 8) for dev in range(8)]))
+    up_delta = jnp.roll(
+        jnp.concatenate(ring[::-1], axis=0), (lax.axis_index("row") + 1) * ring[0].shape[0], axis=0
+    )
     grad_rows = grad_full
     acc_down = lax.dot_general(
         hidden_act, grad_rows, contract_first, preferred_element_type=jnp.float32

time: 583 us -> 561 us (0.962)
  waiting for transfers between devices: 446 us -> 399 us
  local copies, waits for them, and re-layouts: 24.2 us -> 52.5 us
    ppermute x0 -> x7, waiting for transfers between devices: none -> 190 us  [body(): lax.ppermute(ring[-1], 'row', [(dev, (dev + 1) % 8) for dev in range(8)])]
    all_gather x1, waiting for transfers between devices: 78.6 us -> 0.01 us  [body(): gate_delta = lax.all_gather(products[1], 'row', axis=0, tiled=True)]
    all_gather x1 -> x0, waiting for transfers between devices: 67.6 us -> none  [body(): up_delta = lax.all_gather(products[2], 'row', axis=0, tiled=True)]
    reduce_scatter x1, waiting for transfers between devices: 39.7 us -> 0.01 us  [body(): lax.psum_scatter(acc_input, 'col', scatter_dimension=0, tiled=True)]
    all_gather x1, waiting for transfers between devices: 29.8 us -> 0.01 us  [body(): hidden_act = lax.all_gather(products[0], 'row', axis=0, tiled=True)]
    unnamed x10 -> x29, local copies, waits for them, and re-layouts: 24.2 us -> 51.5 us
    all_gather x1, waiting for transfers between devices: 19.8 us -> 0.02 us  [body(): lax.all_gather(activations, 'col', axis=0, tiled=True)]
  transfers between devices with their start and end apart: 7 -> 13, of which waited for: 7 -> 9; matrix products, arithmetic and copies ran while one was open for 17% -> 22% of each run, Pallas kernels for 0% -> 0%
where the time goes in v1:
time: 561 us; the launch traced here: 560 us
  waiting for transfers between devices  399 us (71%)
  matrix products  88 us (16%)
  local copies, waits for them, and re-layouts  52.5 us (9%)
  between operations  14.2 us (3%)
  other arithmetic  6.23 us (1%)
    ppermute x7, waiting for transfers between devices, body(): lax.ppermute(ring[-1], 'row', [(dev, (dev + 1) % 8) for dev in range(8)])  190 us
    reduce_scatter x1, waiting for transfers between devices, body(): lax.psum_scatter(lax.dot_general(grad_rows, down_weight, contract_last, p...  168 us
    unnamed x29, local copies, waits for them, and re-layouts  51.5 us
    all_gather x1, waiting for transfers between devices, body(): lax.all_gather(out_grad, 'col', axis=0, tiled=True)  39.9 us
    dot_general x1, matrix products, body(): lax.dot_general(grad_rows, down_weight, contract_last, preferred_element_...  16 us
    dot_general x1, matrix products, body(): lax.dot_general(up_delta, up_weight, contract_last, preferred_element_typ...  15.2 us
    dot_general x1, matrix products, body(): lax.dot_general(act_full, up_delta, contract_first, preferred_element_typ...  14.9 us
    dot_general x1, matrix products, body(): lax.dot_general(act_full, gate_delta, contract_first, preferred_element_t...  14.7 us
  transfers between devices with their start and end apart: 13, of which 9 were waited for; matrix products, arithmetic and copies ran while one was open for 22% of the time, Pallas kernels for 0%

profile of v1, /device:TPU:0, one launch (start us, length us, event | category | flops | bytes accessed | tf_op | source)
XLA Modules:
  0.0 560.4 jit_solution(3883867988134683051)
XLA Ops:
  7.9 39.9 %all-gather.5.cloned.1.call-done = bf16[1024,1024]{1,0:T(8,128)(2,1)} async-done(((bf16[256,1024]{1,0:T(8,128)(2,1)}), bf16[1024,1024]{1,0:T(8,128)(2,1)}) %all-gather.5.cloned.1.call-update) | async-done | bytes 2097168 | tf_op jit(solution)/shard_map/all_gather | solution.py:23
  47.9 16.0 %fusion.20 = f32[1024,4096]{1,0:T(8,128)} fusion(bf16[1024,1024]{1,0:T(8,128)(2,1)} %all-gather.5.cloned.1.call-done, bf16[4096,1024]{1,0:T(8,128)(2,1)} %param.13), kind=kOutput, calls=%fused_computation.41 | convolution fusion | flops 8589934592 | bytes 27262976 | tf_op jit(solution)/shard_map/dot_general | solution.py:30
  64.0 168.3 %reduce-scatter.3.cloned.1.call-done = f32[128,4096]{1,0:T(8,128)} async-done(((f32[1024,4096]{1,0:T(8,128)}), f32[128,4096]{1,0:T(8,128)}) %reduce-scatter.3.cloned.1.call-update) | async-done | bytes 2097168 | tf_op jit(solution)/shard_map/reduce_scatter | solution.py:29
  232.4 4.1 multiply_convert_fusion.3
  236.6 25.6 %collective-permute-done = bf16[128,4096]{1,0:T(8,128)(2,1)S(1)} collective-permute-done((bf16[128,4096]{1,0:T(8,128)(2,1)S(1)}, bf16[128,4096]{1,0:T(8,128)(2,1)S(1)}, u32[]{:S(2)}, u32[]{:S(2)}) %collective-permute-start) | collective-permute-done | bytes 1048608 | tf_op jit(solution)/shard_map/ppermute | solution.py:40
  262.3 38.4 %collective-permute-done.1 = bf16[128,4096]{1,0:T(8,128)(2,1)S(1)} collective-permute-done((bf16[128,4096]{1,0:T(8,128)(2,1)S(1)}, bf16[128,4096]{1,0:T(8,128)(2,1)S(1)}, u32[]{:S(2)}, u32[]{:S(2)}) %collective-permute-start.1) | collective-permute-done | bytes 1048608 | tf_op jit(solution)/shard_map/ppermute | solution.py:40
  300.7 38.5 %collective-permute-done.2 = bf16[128,4096]{1,0:T(8,128)(2,1)S(1)} collective-permute-done((bf16[128,4096]{1,0:T(8,128)(2,1)S(1)}, bf16[128,4096]{1,0:T(8,128)(2,1)S(1)}, u32[]{:S(2)}, u32[]{:S(2)}) %collective-permute-start.2) | collective-permute-done | bytes 1048608 | tf_op jit(solution)/shard_map/ppermute | solution.py:40
  340.2 16.1 %collective-permute-done.3 = bf16[128,4096]{1,0:T(8,128)(2,1)} collective-permute-done((bf16[128,4096]{1,0:T(8,128)(2,1)S(1)}, bf16[128,4096]{1,0:T(8,128)(2,1)}, u32[]{:S(2)}, u32[]{:S(2)}) %collective-permute-start.3) | collective-permute-done | bytes 1048608 | tf_op jit(solution)/shard_map/ppermute | solution.py:40
  356.4 16.3 %collective-permute-done.4 = bf16[128,4096]{1,0:T(8,128)(2,1)} collective-permute-done((bf16[128,4096]{1,0:T(8,128)(2,1)}, bf16[128,4096]{1,0:T(8,128)(2,1)}, u32[]{:S(2)}, u32[]{:S(2)}) %collective-permute-start.4) | collective-permute-done | bytes 1048608 | tf_op jit(solution)/shard_map/ppermute | solution.py:40
  372.6 16.3 %collective-permute-done.5 = bf16[128,4096]{1,0:T(8,128)(2,1)} collective-permute-done((bf16[128,4096]{1,0:T(8,128)(2,1)}, bf16[128,4096]{1,0:T(8,128)(2,1)}, u32[]{:S(2)}, u32[]{:S(2)}) %collective-permute-start.5) | collective-permute-done | bytes 1048608 | tf_op jit(solution)/shard_map/ppermute | solution.py:40
  389.0 38.8 %collective-permute-done.6 = bf16[128,4096]{1,0:T(8,128)(2,1)} collective-permute-done((bf16[128,4096]{1,0:T(8,128)(2,1)}, bf16[128,4096]{1,0:T(8,128)(2,1)}, u32[]{:S(2)}, u32[]{:S(2)}) %collective-permute-start.6) | collective-permute-done | bytes 1048608 | tf_op jit(solution)/shard_map/ppermute | solution.py:40
  427.8 2.4 constant_dynamic-update-slice_fusion.15
  430.2 2.3 constant_dynamic-update-slice_fusion.14
  432.4 2.3 constant_dynamic-update-slice_fusion.13
  434.7 2.3 constant_dynamic-update-slice_fusion.12
  437.0 1.1 constant_dynamic-update-slice_fusion.11
  440.2 1.2 constant_dynamic-update-slice_fusion.8
  441.4 2.4 constant_dynamic-update-slice_fusion.7
  443.8 2.3 constant_dynamic-update-slice_fusion.6
  446.1 2.3 constant_dynamic-update-slice_fusion.5
  448.4 2.3 constant_dynamic-update-slice_fusion.4
  450.7 1.1 constant_dynamic-update-slice_fusion.3
  452.9 1.1 constant_dynamic-update-slice_fusion.1
  453.9 1.1 constant_dynamic-update-slice_fusion
  455.0 12.7 %fusion.21 = f32[1024,1024]{1,0:T(8,128)S(1)} fusion(bf16[1024,4096]{1,0:T(8,128)(2,1)} %all-gather.7.cloned.1.call-done, bf16[1024,4096]{1,0:T(8,128)(2,1)} %param.11), kind=kOutput, calls=%fused_computation.42 | convolution fusion | flops 8589934592 | bytes 20971520 | tf_op jit(solution)/shard_map/dot_general | solution.py:52
  467.7 15.2 %fusion.15 = f32[1024,1024]{1,0:T(8,128)} fusion(f32[1024,1024]{1,0:T(8,128)S(1)} %fusion.21, bf16[1024,4096]{1,0:T(8,128)(2,1)} %param.12, bf16[2048,4096]{1,0:T(8,128)(2,1)} %constant_dynamic-update-slice_fusion, s32[]{:T(128)S(6)} %select_n.14), kind=kOutput, calls=%fused_computation.22 | convolution fusion | flops 8590983168 | bytes 25165828 | tf_op jit(solution)/shard_map/dot_general | solution.py:55
  482.9 14.9 %fusion.4 = bf16[1024,4096]{0,1:T(8,128)(2,1)} fusion(bf16[1024,1024]{1,0:T(8,128)(2,1)} %all-gather.9.cloned.1.call-done, bf16[2048,4096]{1,0:T(8,128)(2,1)} %constant_dynamic-update-slice_fusion, s32[]{:T(128)S(6)} %select_n.14), kind=kOutput, calls=%fused_computation.7 | convolution fusion | flops 8598323200 | bytes 18874372 | tf_op jit(solution)/shard_map/dot_general | solution.py:51
  497.9 12.2 %copy.12 = bf16[1024,4096]{1,0:T(8,128)(2,1)} copy(bf16[1024,4096]{0,1:T(8,128)(2,1)} %fusion.4) | data formatting | bytes 16777216
  510.0 14.7 %fusion.3 = bf16[1024,4096]{0,1:T(8,128)(2,1)} fusion(bf16[1024,4096]{1,0:T(8,128)(2,1)} %all-gather.7.cloned.1.call-done, bf16[1024,1024]{1,0:T(8,128)(2,1)S(1)} %copy-done.5), kind=kOutput, calls=%fused_computation.6 | convolution fusion | flops 8598323200 | bytes 18874368 | tf_op jit(solution)/shard_map/dot_general | solution.py:48
  524.7 12.1 %copy.11 = bf16[1024,4096]{1,0:T(8,128)(2,1)} copy(bf16[1024,4096]{0,1:T(8,128)(2,1)} %fusion.3) | data formatting | bytes 16777216
  536.8 14.6 %multiply_convert_fusion = bf16[4096,1024]{1,0:T(8,128)(2,1)} fusion(bf16[1024,4096]{1,0:T(8,128)(2,1)} %all-gather.11.cloned.1.call-done, bf16[1024,1024]{1,0:T(8,128)(2,1)S(1)} %copy-done.4), kind=kOutput, calls=%fused_computation | convolution fusion | flops 8598323200 | bytes 18874368 | tf_op jit(solution)/shard_map/dot_general | solution.py:45
  551.4 2.1 convert_element_type.37
  (38 shorter events, 5.2 us)
Async XLA Ops:
  7.2 40.7 %all-gather.5.cloned.1.call-start = ((), (), s32[]{:S(2)}) async-start(), calls=%async_computation.2 | async-start | bytes 2621440 | tf_op jit(solution)/shard_map/all_gather | solution.py:23
  7.9 224.5 %reduce-scatter.3.cloned.1.call-start = ((), (), s32[]{:S(2)}) async-start(), calls=%async_computation.3 | async-start | bytes 18874368 | tf_op jit(solution)/shard_map/reduce_scatter | solution.py:29
  63.9 168.4 %copy-start.2 = (bf16[128,4096]{1,0:T(8,128)(2,1)S(1)}, bf16[128,4096]{1,0:T(8,128)(2,1)}, u32[]{:S(2)}) copy-start(bf16[128,4096]{1,0:T(8,128)(2,1)} %param.9) | copy-start | bytes 3145732
  63.9 168.4 %copy-start.3 = (bf16[128,4096]{1,0:T(8,128)(2,1)S(1)}, bf16[128,4096]{1,0:T(8,128)(2,1)}, u32[]{:S(2)}) copy-start(bf16[128,4096]{1,0:T(8,128)(2,1)} %param.10) | copy-start | bytes 3145732
  64.0 391.1 %all-gather.7.cloned.1.call-start = ((), (), s32[]{:S(2)}) async-start(), calls=%async_computation.4 | async-start | bytes 9437184 | tf_op jit(solution)/shard_map/all_gather | solution.py:37
  236.5 246.4 %all-gather.9.cloned.1.call-start = ((), (), s32[]{:S(2)}) async-start(), calls=%async_computation.6 | async-start | bytes 2621440 | tf_op jit(solution)/shard_map/all_gather | solution.py:22
  236.6 25.7 %collective-permute-start = (bf16[128,4096]{1,0:T(8,128)(2,1)S(1)}, bf16[128,4096]{1,0:T(8,128)(2,1)S(1)}, u32[]{:S(2)}, u32[]{:S(2)}) collective-permute-start(bf16[128,4096]{1,0:T(8,128)(2,1)S(1)} %get-tuple-element.8), channel_id=1, source_target_pairs={{0,4},{4,8},{8,12},{12,16},{16,20},{20,24},{24,28},{28,0},{1,5},{5... | collective-permute-start | bytes 3145736 | tf_op jit(solution)/shard_map/ppermute | solution.py:40
  262.2 38.5 %collective-permute-start.1 = (bf16[128,4096]{1,0:T(8,128)(2,1)S(1)}, bf16[128,4096]{1,0:T(8,128)(2,1)S(1)}, u32[]{:S(2)}, u32[]{:S(2)}) collective-permute-start(bf16[128,4096]{1,0:T(8,128)(2,1)S(1)} %collective-permute-done), channel_id=1, source_target_pairs={{0,4},{4,8},{8,12},{12,16},{16,20},{20,24},{24,28},{28,0},{1,5},{5... | collective-permute-start | bytes 3145736 | tf_op jit(solution)/shard_map/ppermute | solution.py:40
  262.3 274.6 %all-gather.11.cloned.1.call-start = ((), (), s32[]{:S(2)}) async-start(), calls=%async_computation.7 | async-start | bytes 9437184 | tf_op jit(solution)/shard_map/all_gather | solution.py:36
  300.7 38.5 %collective-permute-start.2 = (bf16[128,4096]{1,0:T(8,128)(2,1)S(1)}, bf16[128,4096]{1,0:T(8,128)(2,1)S(1)}, u32[]{:S(2)}, u32[]{:S(2)}) collective-permute-start(bf16[128,4096]{1,0:T(8,128)(2,1)S(1)} %collective-permute-done.1), channel_id=1, source_target_pairs={{0,4},{4,8},{8,12},{12,16},{16,20},{20,24},{24,28},{28,0},{1,5},{5... | collective-permute-start | bytes 3145736 | tf_op jit(solution)/shard_map/ppermute | solution.py:40
  339.2 1.0 copy-start
  340.2 16.1 %collective-permute-start.3 = (bf16[128,4096]{1,0:T(8,128)(2,1)S(1)}, bf16[128,4096]{1,0:T(8,128)(2,1)}, u32[]{:S(2)}, u32[]{:S(2)}) collective-permute-start(bf16[128,4096]{1,0:T(8,128)(2,1)S(1)} %collective-permute-done.2), channel_id=1, source_target_pairs={{0,4},{4,8},{8,12},{12,16},{16,20},{20,24},{24,28},{28,0},{1,5},{5... | collective-permute-start | bytes 3145736 | tf_op jit(solution)/shard_map/ppermute | solution.py:40
  356.3 16.3 %collective-permute-start.4 = (bf16[128,4096]{1,0:T(8,128)(2,1)}, bf16[128,4096]{1,0:T(8,128)(2,1)}, u32[]{:S(2)}, u32[]{:S(2)}) collective-permute-start(bf16[128,4096]{1,0:T(8,128)(2,1)} %collective-permute-done.3), channel_id=1, source_target_pairs={{0,4},{4,8},{8,12},{12,16},{16,20},{20,24},{24,28},{28,0},{1,5},{5... | collective-permute-start | bytes 3145736 | tf_op jit(solution)/shard_map/ppermute | solution.py:40
  356.3 195.1 %reduce-scatter.5.cloned.1.call-start = ((), (), s32[]{:S(2)}) async-start(), calls=%async_computation.5 | async-start | bytes 5242880 | tf_op jit(solution)/shard_map/reduce_scatter | solution.py:61
  372.6 16.3 %collective-permute-start.5 = (bf16[128,4096]{1,0:T(8,128)(2,1)}, bf16[128,4096]{1,0:T(8,128)(2,1)}, u32[]{:S(2)}, u32[]{:S(2)}) collective-permute-start(bf16[128,4096]{1,0:T(8,128)(2,1)} %collective-permute-done.4), channel_id=1, source_target_pairs={{0,4},{4,8},{8,12},{12,16},{16,20},{20,24},{24,28},{28,0},{1,5},{5... | collective-permute-start | bytes 3145736 | tf_op jit(solution)/shard_map/ppermute | solution.py:40
  389.0 38.8 %collective-permute-start.6 = (bf16[128,4096]{1,0:T(8,128)(2,1)}, bf16[128,4096]{1,0:T(8,128)(2,1)}, u32[]{:S(2)}, u32[]{:S(2)}) collective-permute-start(bf16[128,4096]{1,0:T(8,128)(2,1)} %collective-permute-done.5), channel_id=1, source_target_pairs={{0,4},{4,8},{8,12},{12,16},{16,20},{20,24},{24,28},{28,0},{1,5},{5... | collective-permute-start | bytes 3145736 | tf_op jit(solution)/shard_map/ppermute | solution.py:40
  389.0 48.1 %copy-start.1 = (bf16[128,4096]{1,0:T(8,128)(2,1)S(1)}, bf16[128,4096]{1,0:T(8,128)(2,1)}, u32[]{:S(2)}) copy-start(bf16[128,4096]{1,0:T(8,128)(2,1)} %copy-done) | copy-start | bytes 3145732
  497.9 12.2 %copy-start.5 = (bf16[1024,1024]{1,0:T(8,128)(2,1)S(1)}, bf16[1024,1024]{1,0:T(8,128)(2,1)}, u32[]{:S(2)}) copy-start(bf16[1024,1024]{1,0:T(8,128)(2,1)} %all-gather.9.cloned.1.call-done) | copy-start | bytes 6291460
  524.7 12.1 %copy-start.4 = (bf16[1024,1024]{1,0:T(8,128)(2,1)S(1)}, bf16[1024,1024]{1,0:T(8,128)(2,1)}, u32[]{:S(2)}) copy-start(bf16[1024,1024]{1,0:T(8,128)(2,1)} %all-gather.5.cloned.1.call-done) | copy-start | bytes 6291460
Sparse Core Ops, SparseCore 0:
  9.8 38.0 all-gather.4
  64.1 168.2 reduce-scatter.2
  236.6 107.5 all-gather.6
  346.0 33.5 all-gather.8
  381.0 93.1 all-gather.10
  483.0 50.8 reduce-scatter.4
